TPU v7x, 256 devices: a whole 4x4x8 slice. The times are simulated.
256 devices in a mesh: dp: 32 (over z, x_hi, core), tm: 8 (over y, x_lo).
Axes of the slice: x: 4 (x_hi: 2, x_lo: 2; x = x_hi * 2 + x_lo), y: 4, z: 8, core: 2. Of those that a mesh axis runs over, the one named last changes fastest.
Arguments:
- queries: bfloat16 [32, 3072, 256], P('dp', 'tm'), may hold values from -6 to 6
- key_input: bfloat16 [32, 3072, 256], P('dp', 'tm'), may hold values from -6 to 6
- value_input: bfloat16 [32, 3072, 256], P('dp', 'tm'), may hold values from -6 to 6
- lengths: int32 [32], P('dp'), may hold values from 1536 to 3072, as said below
- projection: bfloat16 [4096, 256], P('dp'), may hold values from -0.09375 to 0.09375
- upstream: bfloat16 [32, 3072, 4096], P('dp', 'tm'), may hold values from -6 to 6
- glu_input: bfloat16 [32, 3072, 4096], P('dp', 'tm'), may hold values from -6 to 6
- kernel: bfloat16 [2048, 31], P('dp'), may hold values from -1 to 1
- norm_gain: bfloat16 [2048], P('dp'), may hold values from 0.5 to 1.5
- conv_upstream: bfloat16 [32, 3072, 2048], P('dp', 'tm'), may hold values from -6 to 6
Outputs:
- grad_queries: bfloat16 [32, 3072, 256], P('dp', 'tm')
- grad_keys: bfloat16 [32, 3072, 256], P('dp', 'tm')
- grad_values: bfloat16 [32, 3072, 256], P('dp', 'tm')
- grad_projection: bfloat16 [4096, 256], P('dp')
- grad_glu: bfloat16 [32, 3072, 4096], P('dp', 'tm')
- grad_kernel: float32 [2048, 31], P('dp')
- grad_gain: float32 [2048], P('dp')
Inputs may be any that keep to these rules, and one draw needn't show every extreme that they name: `lengths`: the valid frames of an utterance are its first ones; one utterance has all 3072 valid and one exactly 1536.
All inputs are finite; a program needn't handle non-finite values.
Results may differ from a plain program's by a relative error of at most 0.02.
Values may be sent and summed in bfloat16 or wider, within the bound.
No kernel may reach another device: no remote copies, remote signals or barrier semaphores. Data moves between devices by JAX's collectives and lax.ppermute only.
A program may use at most 128 MiB of HBM per device.

v0:
```python
import jax
import jax.numpy as jnp
from jax import lax
from jax.sharding import PartitionSpec as P

HEADS = 2
HDIM = 128
CH = 2048
KW = 31
NEG_FILL = -1e30
NORM_EPS = 1e-05


def from_behind(block, axis, distance):
    devices = range(lax.axis_size(axis))
    route = [((i - distance) % len(devices), i) for i in devices]
    return lax.ppermute(block, axis, route)


def extended(cells, sides, width):
    for axis, dim in sides:
        count = lax.axis_size(axis)
        ends = count - 1
        head = lax.slice_in_dim(cells, 0, width, axis=dim)
        tail = lax.slice_in_dim(cells, cells.shape[dim] - width, cells.shape[dim], axis=dim)
        cells = jnp.concatenate(
            [
                lax.ppermute(tail, axis, [(i, (i + 1) % count) for i in range(ends)]),
                cells,
                lax.ppermute(head, axis, [((i + 1) % count, i) for i in range(ends)]),
            ],
            axis=dim,
        )
    return cells


def depthwise(padded, kernel_f, frame_rows):
    mixed = jnp.zeros((frame_rows, kernel_f.shape[0]), jnp.float32)
    for tap in range(kernel_f.shape[1]):
        mixed = mixed + padded[tap : tap + frame_rows].astype(jnp.float32) * kernel_f[:, tap]
    return mixed


def back_depthwise(grad_pad, kernel_f, frame_rows):
    half_width = (kernel_f.shape[1] - 1) // 2
    result = jnp.zeros((frame_rows, kernel_f.shape[0]), jnp.float32)
    for tap in range(kernel_f.shape[1]):
        begin = 2 * half_width - tap
        result = (
            result + grad_pad[begin : begin + frame_rows].astype(jnp.float32) * kernel_f[:, tap]
        )
    return result


def tap_products(grad_low, padded, frame_rows, tap_count):
    grad_f = grad_low.astype(jnp.float32)
    return jnp.stack(
        [
            jnp.sum(grad_f * padded[tap : tap + frame_rows].astype(jnp.float32), axis=0)
            for tap in range(tap_count)
        ],
        axis=1,
    )


def norm_backward(mixed, gain_f, cotangent, frame_live):
    centre = mixed - jnp.mean(mixed, axis=-1, keepdims=True)
    inv_std = lax.rsqrt(jnp.mean(centre * centre, axis=-1, keepdims=True) + NORM_EPS)
    standard = centre * inv_std
    normed = standard * gain_f
    squash = jax.nn.sigmoid(normed)
    grad_normed = (
        cotangent.astype(jnp.float32) * frame_live * (squash + normed * squash * (1.0 - squash))
    )
    gain_term = jnp.sum(grad_normed * standard, axis=0)
    scaled = grad_normed * gain_f
    grad_conv = inv_std * (
        scaled
        - jnp.mean(scaled, axis=-1, keepdims=True)
        - standard * jnp.mean(scaled * standard, axis=-1, keepdims=True)
    )
    return (grad_conv.astype(jnp.bfloat16), gain_term)


def per_device(
    queries,
    key_input,
    value_input,
    lengths,
    projection,
    upstream,
    glu_input,
    kernel,
    norm_gain,
    conv_upstream,
):
    time_count = lax.axis_size("tm")
    time_rank = lax.axis_index("tm")
    frame_rows = queries.shape[1]
    flat_width = queries.shape[2]
    score_scale = HDIM ** (-0.5)
    length = lengths[0]
    full_proj, full_kernel, full_gain = (
        lax.all_gather(projection, "dp", axis=0, tiled=True),
        lax.all_gather(kernel, "dp", axis=0, tiled=True),
        lax.all_gather(norm_gain, "dp", axis=0, tiled=True),
    )
    query_heads = queries[0].reshape(frame_rows, HEADS, HDIM)
    key_heads = key_input[0].reshape(frame_rows, HEADS, HDIM)
    value_heads = value_input[0].reshape(frame_rows, HEADS, HDIM)

    def block_scores(key_block, key_offset):
        scores = (
            jnp.einsum("qhd,khd->hqk", query_heads, key_block, preferred_element_type=jnp.float32)
            * score_scale
        )
        key_live = key_offset + jnp.arange(key_block.shape[0], dtype=jnp.int32) < length
        return jnp.where(key_live[None, None, :], scores, NEG_FILL)

    def absorb(state_now, key_block, value_block, key_offset):
        run_top, run_total, run_acc = state_now
        scores = block_scores(key_block, key_offset)
        new_top = jnp.maximum(run_top, jnp.max(scores, axis=-1))
        factor = jnp.exp(run_top - new_top)
        weights = jnp.exp(scores - new_top[:, :, None])
        run_total = run_total * factor + jnp.sum(weights, axis=-1)
        contrib = jnp.einsum(
            "hqk,khd->qhd",
            weights,
            value_block.astype(jnp.float32),
            precision=lax.Precision.HIGHEST,
        )
        run_acc = run_acc * jnp.transpose(factor)[:, :, None] + contrib
        return (new_top, run_total, run_acc)

    start_state = (
        jnp.full((HEADS, frame_rows), NEG_FILL, jnp.float32),
        jnp.zeros((HEADS, frame_rows), jnp.float32),
        jnp.zeros((frame_rows, HEADS, HDIM), jnp.float32),
    )

    def forward_step(step, loop_state):
        key_block, value_block, inner = loop_state
        source = (time_rank - step) % time_count
        inner = absorb(inner, key_block, value_block, source * frame_rows)
        key_block, value_block = from_behind((key_block, value_block), "tm", 1)
        return (key_block, value_block, inner)

    key_block, value_block, inner = lax.fori_loop(
        0, time_count - 1, forward_step, (key_heads, value_heads, start_state)
    )
    source = (time_rank - (time_count - 1)) % time_count
    state_now = absorb(inner, key_block, value_block, source * frame_rows)
    run_top, run_total, run_acc = state_now
    log_total = run_top + jnp.log(run_total)
    attended = (run_acc / jnp.transpose(run_total)[:, :, None]).astype(jnp.bfloat16)
    upstream_rows = upstream[0]
    grad_out = jnp.dot(upstream_rows, full_proj, preferred_element_type=jnp.float32).astype(
        jnp.bfloat16
    )
    grad_heads = grad_out.reshape(frame_rows, HEADS, HDIM)
    row_delta = jnp.einsum("qhd,qhd->hq", grad_heads, attended, preferred_element_type=jnp.float32)

    def backward_block(key_block, value_block, key_offset):
        scores = block_scores(key_block, key_offset)
        weights = jnp.exp(scores - log_total[:, :, None])
        weights_low = weights.astype(jnp.bfloat16)
        add_value = jnp.einsum(
            "hqk,qhd->khd", weights_low, grad_heads, preferred_element_type=jnp.float32
        )
        grad_weights = jnp.einsum(
            "qhd,khd->hqk", grad_heads, value_block, preferred_element_type=jnp.float32
        )
        grad_scores = (weights * (grad_weights - row_delta[:, :, None]) * score_scale).astype(
            jnp.bfloat16
        )
        add_query = jnp.einsum(
            "hqk,khd->qhd", grad_scores, key_block, preferred_element_type=jnp.float32
        )
        add_key = jnp.einsum(
            "hqk,qhd->khd", grad_scores, query_heads, preferred_element_type=jnp.float32
        )
        return (add_query, add_key, add_value)

    zero_heads = jnp.zeros((frame_rows, HEADS, HDIM), jnp.float32)

    def pass_grads(key_acc, value_acc):
        return from_behind((key_acc, value_acc), "tm", 1)

    def backward_step(step, loop_state):
        key_block, value_block, key_acc, value_acc, query_acc = loop_state
        source = (time_rank - step) % time_count
        add_query, add_key, add_value = backward_block(key_block, value_block, source * frame_rows)
        key_acc, value_acc = pass_grads(key_acc + add_key, value_acc + add_value)
        key_block, value_block = from_behind((key_block, value_block), "tm", 1)
        return (key_block, value_block, key_acc, value_acc, query_acc + add_query)

    key_block, value_block, key_acc, value_acc, query_acc = lax.fori_loop(
        0,
        time_count - 1,
        backward_step,
        (key_heads, value_heads, zero_heads, zero_heads, zero_heads),
    )
    source = (time_rank - (time_count - 1)) % time_count
    add_query, add_key, add_value = backward_block(key_block, value_block, source * frame_rows)
    key_acc, value_acc = pass_grads(key_acc + add_key, value_acc + add_value)
    query_acc = query_acc + add_query
    grad_queries = query_acc.reshape(1, frame_rows, flat_width).astype(jnp.bfloat16)
    grad_keys = key_acc.reshape(1, frame_rows, flat_width).astype(jnp.bfloat16)
    grad_values = value_acc.reshape(1, frame_rows, flat_width).astype(jnp.bfloat16)
    half_width = (KW - 1) // 2
    frame_ids = time_rank * frame_rows + jnp.arange(frame_rows, dtype=jnp.int32)
    frame_live = (frame_ids < length).astype(jnp.float32)[:, None]
    glu_rows = glu_input[0]
    linear = glu_rows[:, :CH].astype(jnp.float32)
    gate_sig = jax.nn.sigmoid(glu_rows[:, CH:].astype(jnp.float32))
    activ = (linear * gate_sig * frame_live).astype(jnp.bfloat16)
    padded = extended(activ, (("tm", 0),), half_width)
    kernel_f = full_kernel.astype(jnp.float32)
    gain_f = full_gain.astype(jnp.float32)
    mixed = depthwise(padded, kernel_f, frame_rows)
    grad_conv, gain_term = norm_backward(mixed, gain_f, conv_upstream[0], frame_live)
    grad_pad = extended(grad_conv, (("tm", 0),), half_width)
    kernel_term = tap_products(grad_conv, padded, frame_rows, KW)
    grad_activ = back_depthwise(grad_pad, kernel_f, frame_rows) * frame_live
    first_half = grad_activ * gate_sig
    second_half = grad_activ * linear * gate_sig * (1.0 - gate_sig)
    grad_glu = jnp.concatenate([first_half, second_half], axis=-1).astype(jnp.bfloat16)[None]
    attended_flat = attended.reshape(frame_rows, flat_width)
    proj_part = lax.psum_scatter(
        lax.dot_general(
            upstream_rows,
            attended_flat,
            (((0,), (0,)), ((), ())),
            preferred_element_type=jnp.float32,
        ),
        "dp",
        scatter_dimension=0,
        tiled=True,
    )
    kernel_part, gain_part = (
        lax.psum_scatter(kernel_term, "dp", scatter_dimension=0, tiled=True),
        lax.psum_scatter(gain_term, "dp", scatter_dimension=0, tiled=True),
    )
    proj_total, kernel_total, gain_total = lax.psum((proj_part, kernel_part, gain_part), "tm")
    grad_projection = proj_total.astype(jnp.bfloat16)
    return (
        grad_queries,
        grad_keys,
        grad_values,
        grad_projection,
        grad_glu,
        kernel_total,
        gain_total,
    )


def solution(mesh):
    in_specs = (
        P("dp", "tm", None),
        P("dp", "tm", None),
        P("dp", "tm", None),
        P("dp"),
        P("dp", None),
        P("dp", "tm", None),
        P("dp", "tm", None),
        P("dp", None),
        P("dp"),
        P("dp", "tm", None),
    )
    out_specs = (
        P("dp", "tm", None),
        P("dp", "tm", None),
        P("dp", "tm", None),
        P("dp", None),
        P("dp", "tm", None),
        P("dp", None),
        P("dp"),
    )
    return jax.shard_map(
        per_device, mesh=mesh, in_specs=in_specs, out_specs=out_specs, check_vma=False
    )
```

profile of v0, /device:TPU:4, one launch (start us, length us, event | category | flops | bytes accessed | tf_op | source)
XLA Modules:
  0.0 809.6 jit_solution(5044786274540221472)
XLA Ops:
  17.3 41.1 %all-gather = bf16[32,64,31]{1,2,0:T(8,128)(2,1)S(1)} all-gather(bf16[1,64,31]{1,2,0:T(8,128)(2,1)S(1)} %bitcast.320), channel_id=1, replica_groups=mesh['dp'=32,'tm'=8] {'dp'}, dimensions={0}, use_global_device_ids=true | all-gather | bytes 130944 | tf_op jit(solution)/shard_map/all_gather | solution.py:105
  64.8 64.7 %all-reduce = bf16[2048]{0:T(1024)(128)(2,1)S(1)} all-reduce(bf16[2048]{0:T(1024)(128)(2,1)S(1)} %dynamic-update-slice), channel_id=1, replica_groups=mesh['dp'=32,'tm'=8] {'dp'}, use_global_device_ids=true, to_apply=%add | all-reduce | flops 2048 | bytes 8192
  129.6 43.8 %fusion.190 = (f32[384]{0:T(512)S(1)}, f32[384,2048]{1,0:T(8,128)S(1)}) fusion(f32[2048]{0:T(1024)S(1)} %bitcast.229, bf16[15,2048]{1,0:T(8,128)(2,1)S(1)} %collective-permute-done.9, bf16[384,2048]{1,0:T(8,128)(2,1)} %copy-done.3, f32[2048]{0:T(1024)} %bitcast.231, f32[2048]{0:T(1024)} %bitcast.233, f32[2048]{0:T(1024)} %bitcast.235, f32[2048]{0:T(1024)} %bitcast.237, ...), kind=kLoop, calls=%fused_computation.373 | loop fusion | flops 143916672 | bytes 5096960 | tf_op jit(solution)/shard_map/reduce_sum | solution.py:67
  177.1 12.4 %fusion.98 = (f32[2048]{0:T(1024)}, f32[2048]{0:T(1024)}, f32[2048]{0:T(1024)}, f32[2048]{0:T(1024)}, f32[2048]{0:T(1024)}, /*index=5*/f32[2048]{0:T(1024)}, f32...) fusion(bf16[15,2048]{1,0:T(8,128)(2,1)S(1)} %collective-permute-done.9, ...), kind=kLoop, calls=%fused_computation.234 | loop fusion | flops 49526784 | bytes 9586688 | tf_op jit(solution)/shard_map/reduce_sum | solution.py:59
  189.4 7.3 fusion.97
  196.8 4.7 fusion.82
  201.5 3.6 fusion.81
  205.1 3.5 stack.127
  210.7 9.6 %reduce-scatter.5.cloned.1.call-start = ((), (), s32[]{:S(2)}) async-start(), calls=%async_computation.3 | async-start | bytes 4325376 | tf_op jit(solution)/shard_map/reduce_scatter | solution.py:230
  232.3 88.0 %while.48 = (s32[]{:T(128)}, bf16[384,2,128]{2,0,1:T(8,128)(2,1)}, bf16[384,2,128]{2,0,1:T(8,128)(2,1)}, f32[2,384]{1,0:T(2,128)S(1)}, f32[2,384]{1,0:T(2,128)S(...) while((s32[]{:T(128)}, bf16[384,2,128]{2,0,1:T(8,128)(2,1)}, ...), condition=%wide.region_3.4_spmd.clone, body=%wide.region_0.3_spmd.clone.sunk | while | flops 530552064 | bytes 12043402 | solution.py:149
  242.6 3.2 fusion.255
  255.1 3.3 fusion.255
  266.7 3.3 fusion.255
  270.0 3.3 collective-permute-done
  280.3 3.3 fusion.255
  291.8 3.3 fusion.255
  303.0 3.3 fusion.255
  315.2 3.3 fusion.255
  325.9 5.2 collective-permute-start.11
  334.3 67.0 %all-reduce.1 = f32[2048]{0:T(1024)} all-reduce(f32[2048]{0:T(1024)} %get-tuple-element.705), channel_id=4, replica_groups=mesh['dp'=32,'tm'=8] {'dp'}, use_global_device_ids=true, to_apply=%region_48.49.clone | all-reduce | flops 2048 | bytes 16384
  402.9 46.6 %fusion.104 = (bf16[1,384,2048]{2,1,0:T(8,128)(2,1)S(1)}, f32[384,2048]{1,0:T(8,128)S(1)}) fusion(bf16[384,4096]{1,0:T(8,128)(2,1)} %bitcast.213, f32[384]{0:T(512)S(1)} %copy-done.50, f32[2048]{0:T(1024)S(1)} %bitcast.230, bf16[384,2048]{1,0:T(8,128)(2,1)} %copy-done.5, bf16[15,2048]{1,0:T(8,128)(2,1)} %collective-permute-done.11, f32[2048]{0:T(1024)S(1)} %bitcast.232, ...), kind=kLoop, calls=%fused_computation.250 | loop fusion | flops 148635648 | bytes 8242688 | tf_op jit(solution)/shard_map/concatenate | solution.py:228
  459.1 3.2 convolution_bitcast_fusion.4
  465.0 277.5 %while.49 = (s32[]{:T(128)}, bf16[384,2,128]{2,0,1:T(8,128)(2,1)}, bf16[384,2,128]{2,0,1:T(8,128)(2,1)}, f32[384,2,128]{2,0,1:T(8,128)}, f32[384,2,128]{2,0,1:T(...) while((s32[]{:T(128)}, bf16[384,2,128]{2,0,1:T(8,128)(2,1)}, ...), condition=%wide.region_7.8_spmd.clone, body=%wide.region_6.7_spmd.clone.sunk | while | flops 380240640 | bytes 16915696 | solution.py:198
  482.9 18.6 %collective-permute-done.2 = bf16[384,2,128]{2,0,1:T(8,128)(2,1)} collective-permute-done((bf16[384,2,128]{2,0,1:T(8,128)(2,1)}, bf16[384,2,128]{2,0,1:T(8,128)(2,1)}, u32[]{:S(2)}, u32[]{:S(2)}) %collective-permute-start.2) | collective-permute-done | bytes 196640 | tf_op jit(solution)/shard_map/while/body/eval_jaxpr/ppermute | solution.py:17
  521.2 29.3 %collective-permute-done.2 = bf16[384,2,128]{2,0,1:T(8,128)(2,1)} collective-permute-done((bf16[384,2,128]{2,0,1:T(8,128)(2,1)}, bf16[384,2,128]{2,0,1:T(8,128)(2,1)}, u32[]{:S(2)}, u32[]{:S(2)}) %collective-permute-start.2) | collective-permute-done | bytes 196640 | tf_op jit(solution)/shard_map/while/body/eval_jaxpr/ppermute | solution.py:17
  550.5 3.5 collective-permute-done.3
  569.8 22.1 %collective-permute-done.2 = bf16[384,2,128]{2,0,1:T(8,128)(2,1)} collective-permute-done((bf16[384,2,128]{2,0,1:T(8,128)(2,1)}, bf16[384,2,128]{2,0,1:T(8,128)(2,1)}, u32[]{:S(2)}, u32[]{:S(2)}) %collective-permute-start.2) | collective-permute-done | bytes 196640 | tf_op jit(solution)/shard_map/while/body/eval_jaxpr/ppermute | solution.py:17
  608.4 22.2 %collective-permute-done.2 = bf16[384,2,128]{2,0,1:T(8,128)(2,1)} collective-permute-done((bf16[384,2,128]{2,0,1:T(8,128)(2,1)}, bf16[384,2,128]{2,0,1:T(8,128)(2,1)}, u32[]{:S(2)}, u32[]{:S(2)}) %collective-permute-start.2) | collective-permute-done | bytes 196640 | tf_op jit(solution)/shard_map/while/body/eval_jaxpr/ppermute | solution.py:17
  646.7 21.4 %collective-permute-done.2 = bf16[384,2,128]{2,0,1:T(8,128)(2,1)} collective-permute-done((bf16[384,2,128]{2,0,1:T(8,128)(2,1)}, bf16[384,2,128]{2,0,1:T(8,128)(2,1)}, u32[]{:S(2)}, u32[]{:S(2)}) %collective-permute-start.2) | collective-permute-done | bytes 196640 | tf_op jit(solution)/shard_map/while/body/eval_jaxpr/ppermute | solution.py:17
  684.1 20.5 %collective-permute-done.2 = bf16[384,2,128]{2,0,1:T(8,128)(2,1)} collective-permute-done((bf16[384,2,128]{2,0,1:T(8,128)(2,1)}, bf16[384,2,128]{2,0,1:T(8,128)(2,1)}, u32[]{:S(2)}, u32[]{:S(2)}) %collective-permute-start.2) | collective-permute-done | bytes 196640 | tf_op jit(solution)/shard_map/while/body/eval_jaxpr/ppermute | solution.py:17
  720.7 19.7 %collective-permute-done.2 = bf16[384,2,128]{2,0,1:T(8,128)(2,1)} collective-permute-done((bf16[384,2,128]{2,0,1:T(8,128)(2,1)}, bf16[384,2,128]{2,0,1:T(8,128)(2,1)}, u32[]{:S(2)}, u32[]{:S(2)}) %collective-permute-start.2) | collective-permute-done | bytes 196640 | tf_op jit(solution)/shard_map/while/body/eval_jaxpr/ppermute | solution.py:17
  766.4 35.7 %all-reduce.4 = (bf16[128,256]{0,1:T(8,128)(2,1)S(1)}, f32[64,31]{0,1:T(8,128)}, f32[64]{0:T(128)}) all-reduce(f32[128,256]{0,1:T(8,128)} %reduce-scatter.5.cloned.1.call-done, f32[64,31]{0,1:T(8,128)S(1)} %copy-done.42, f32[64]{0:T(128)} %dynamic-slice.2), channel_id=1, replica_groups=mesh['dp'=32,'tm'=8] {'tm'}, use_global_device_ids=true, to_apply=%region_9.10 | all-reduce | flops 34816 | bytes 212992 | tf_op jit(solution)/shard_map/psum | solution.py:245
  (400 shorter events, 259.9 us)
Async XLA Ops:
  7.2 445.5 %reduce-scatter.7.cloned.1.call-start = ((), (), s32[]{:S(2)}) async-start(), calls=%async_computation.4 | async-start | bytes 1081344
  12.9 116.7 %collective-permute-start.8 = (bf16[15,2048]{1,0:T(8,128)(2,1)}, bf16[15,2048]{1,0:T(8,128)(2,1)S(1)}, u32[]{:S(2)}, u32[]{:S(2)}) collective-permute-start(bf16[15,2048]{1,0:T(8,128)(2,1)} %get-tuple-element.798), channel_id=1, source_target_pairs={{0,1},{1,2},{2,3},{3,4},{4,5},{5,6},{6,7},{8,9},{9,10},{10,11},{11... | collective-permute-start | bytes 184328 | tf_op jit(solution)/shard_map/ppermute | solution.py:28
  16.0 113.6 %collective-permute-start.9 = (bf16[15,2048]{1,0:T(8,128)(2,1)}, bf16[15,2048]{1,0:T(8,128)(2,1)S(1)}, u32[]{:S(2)}, u32[]{:S(2)}) collective-permute-start(bf16[15,2048]{1,0:T(8,128)(2,1)} %get-tuple-element.799), channel_id=1, source_target_pairs={{1,0},{2,1},{3,2},{4,3},{5,4},{6,5},{7,6},{9,8},{10,9},{11,10},{12... | collective-permute-start | bytes 184328 | tf_op jit(solution)/shard_map/ppermute | solution.py:30
  209.9 244.2 %all-gather.3.cloned.1.call-start = ((), (), s32[]{:S(2)}) async-start(), calls=%async_computation.2 | async-start | bytes 2162688 | tf_op jit(solution)/shard_map/all_gather | solution.py:104
  210.7 555.7 %reduce-scatter.5.cloned.1.call-start = ((), (), s32[]{:S(2)}) async-start(), calls=%async_computation.3 | async-start | bytes 4325376 | tf_op jit(solution)/shard_map/reduce_scatter | solution.py:230
  324.7 78.0 %collective-permute-start.10 = (bf16[15,2048]{1,0:T(8,128)(2,1)}, bf16[15,2048]{1,0:T(8,128)(2,1)}, u32[]{:S(2)}, u32[]{:S(2)}) collective-permute-start(bf16[15,2048]{1,0:T(8,128)(2,1)} %get-tuple-element.796), channel_id=1, source_target_pairs={{1,0},{2,1},{3,2},{4,3},{5,4},{6,5},{7,6},{9,8},{10,9},{11,10},{12... | collective-permute-start | bytes 184328 | tf_op jit(solution)/shard_map/ppermute | solution.py:30
  325.9 76.7 %collective-permute-start.11 = (bf16[15,2048]{1,0:T(8,128)(2,1)}, bf16[15,2048]{1,0:T(8,128)(2,1)}, u32[]{:S(2)}, u32[]{:S(2)}) collective-permute-start(bf16[15,2048]{1,0:T(8,128)(2,1)} %get-tuple-element.797), channel_id=1, source_target_pairs={{0,1},{1,2},{2,3},{3,4},{4,5},{5,6},{6,7},{8,9},{9,10},{10,11},{11... | collective-permute-start | bytes 184328 | tf_op jit(solution)/shard_map/ppermute | solution.py:28
  474.5 30.1 %collective-permute-start.4 = (f32[384,2,128]{2,0,1:T(8,128)}, f32[384,2,128]{2,0,1:T(8,128)}, u32[]{:S(2)}, u32[]{:S(2)}) collective-permute-start(f32[384,2,128]{2,0,1:T(8,128)} %fusion.268), channel_id=1, source_target_pairs={{7,0},{0,1},{1,2},{2,3},{3,4},{4,5},{5,6},{6,7},{15,8},{8,9},{9,10... | collective-permute-start | bytes 1179656 | tf_op jit(solution)/shard_map/while/body/eval_jaxpr/ppermute | solution.py:17
  476.6 28.0 %collective-permute-start.5 = (f32[384,2,128]{2,0,1:T(8,128)}, f32[384,2,128]{2,0,1:T(8,128)}, u32[]{:S(2)}, u32[]{:S(2)}) collective-permute-start(f32[384,2,128]{2,0,1:T(8,128)} %fusion.269), channel_id=1, source_target_pairs={{7,0},{0,1},{1,2},{2,3},{3,4},{4,5},{5,6},{6,7},{15,8},{8,9},{9,10... | collective-permute-start | bytes 1179656 | tf_op jit(solution)/shard_map/while/body/eval_jaxpr/ppermute | solution.py:17
  477.0 24.5 %collective-permute-start.2 = (bf16[384,2,128]{2,0,1:T(8,128)(2,1)}, bf16[384,2,128]{2,0,1:T(8,128)(2,1)}, u32[]{:S(2)}, u32[]{:S(2)}) collective-permute-start(bf16[384,2,128]{2,0,1:T(8,128)(2,1)} %copy.191), channel_id=1, source_target_pairs={{7,0},{0,1},{1,2},{2,3},{3,4},{4,5},{5,6},{6,7},{15,8},{8,9},{9,10... | collective-permute-start | bytes 589832 | tf_op jit(solution)/shard_map/while/body/eval_jaxpr/ppermute | solution.py:17
  479.0 25.6 %collective-permute-start.3 = (bf16[384,2,128]{2,0,1:T(8,128)(2,1)}, bf16[384,2,128]{2,0,1:T(8,128)(2,1)}, u32[]{:S(2)}, u32[]{:S(2)}) collective-permute-start(bf16[384,2,128]{2,0,1:T(8,128)(2,1)} %copy.192), channel_id=1, source_target_pairs={{7,0},{0,1},{1,2},{2,3},{3,4},{4,5},{5,6},{6,7},{15,8},{8,9},{9,10... | collective-permute-start | bytes 589832 | tf_op jit(solution)/shard_map/while/body/eval_jaxpr/ppermute | solution.py:17
  514.1 39.9 %collective-permute-start.4 = (f32[384,2,128]{2,0,1:T(8,128)}, f32[384,2,128]{2,0,1:T(8,128)}, u32[]{:S(2)}, u32[]{:S(2)}) collective-permute-start(f32[384,2,128]{2,0,1:T(8,128)} %fusion.268), channel_id=1, source_target_pairs={{7,0},{0,1},{1,2},{2,3},{3,4},{4,5},{5,6},{6,7},{15,8},{8,9},{9,10... | collective-permute-start | bytes 1179656 | tf_op jit(solution)/shard_map/while/body/eval_jaxpr/ppermute | solution.py:17
  516.2 37.8 %collective-permute-start.5 = (f32[384,2,128]{2,0,1:T(8,128)}, f32[384,2,128]{2,0,1:T(8,128)}, u32[]{:S(2)}, u32[]{:S(2)}) collective-permute-start(f32[384,2,128]{2,0,1:T(8,128)} %fusion.269), channel_id=1, source_target_pairs={{7,0},{0,1},{1,2},{2,3},{3,4},{4,5},{5,6},{6,7},{15,8},{8,9},{9,10... | collective-permute-start | bytes 1179656 | tf_op jit(solution)/shard_map/while/body/eval_jaxpr/ppermute | solution.py:17
  516.2 34.3 %collective-permute-start.2 = (bf16[384,2,128]{2,0,1:T(8,128)(2,1)}, bf16[384,2,128]{2,0,1:T(8,128)(2,1)}, u32[]{:S(2)}, u32[]{:S(2)}) collective-permute-start(bf16[384,2,128]{2,0,1:T(8,128)(2,1)} %copy.191), channel_id=1, source_target_pairs={{7,0},{0,1},{1,2},{2,3},{3,4},{4,5},{5,6},{6,7},{15,8},{8,9},{9,10... | collective-permute-start | bytes 589832 | tf_op jit(solution)/shard_map/while/body/eval_jaxpr/ppermute | solution.py:17
  516.2 37.8 %collective-permute-start.3 = (bf16[384,2,128]{2,0,1:T(8,128)(2,1)}, bf16[384,2,128]{2,0,1:T(8,128)(2,1)}, u32[]{:S(2)}, u32[]{:S(2)}) collective-permute-start(bf16[384,2,128]{2,0,1:T(8,128)(2,1)} %copy.192), channel_id=1, source_target_pairs={{7,0},{0,1},{1,2},{2,3},{3,4},{4,5},{5,6},{6,7},{15,8},{8,9},{9,10... | collective-permute-start | bytes 589832 | tf_op jit(solution)/shard_map/while/body/eval_jaxpr/ppermute | solution.py:17
  563.5 31.1 %collective-permute-start.4 = (f32[384,2,128]{2,0,1:T(8,128)}, f32[384,2,128]{2,0,1:T(8,128)}, u32[]{:S(2)}, u32[]{:S(2)}) collective-permute-start(f32[384,2,128]{2,0,1:T(8,128)} %fusion.268), channel_id=1, source_target_pairs={{7,0},{0,1},{1,2},{2,3},{3,4},{4,5},{5,6},{6,7},{15,8},{8,9},{9,10... | collective-permute-start | bytes 1179656 | tf_op jit(solution)/shard_map/while/body/eval_jaxpr/ppermute | solution.py:17
  565.6 28.9 %collective-permute-start.5 = (f32[384,2,128]{2,0,1:T(8,128)}, f32[384,2,128]{2,0,1:T(8,128)}, u32[]{:S(2)}, u32[]{:S(2)}) collective-permute-start(f32[384,2,128]{2,0,1:T(8,128)} %fusion.269), channel_id=1, source_target_pairs={{7,0},{0,1},{1,2},{2,3},{3,4},{4,5},{5,6},{6,7},{15,8},{8,9},{9,10... | collective-permute-start | bytes 1179656 | tf_op jit(solution)/shard_map/while/body/eval_jaxpr/ppermute | solution.py:17
  565.6 26.3 %collective-permute-start.2 = (bf16[384,2,128]{2,0,1:T(8,128)(2,1)}, bf16[384,2,128]{2,0,1:T(8,128)(2,1)}, u32[]{:S(2)}, u32[]{:S(2)}) collective-permute-start(bf16[384,2,128]{2,0,1:T(8,128)(2,1)} %copy.191), channel_id=1, source_target_pairs={{7,0},{0,1},{1,2},{2,3},{3,4},{4,5},{5,6},{6,7},{15,8},{8,9},{9,10... | collective-permute-start | bytes 589832 | tf_op jit(solution)/shard_map/while/body/eval_jaxpr/ppermute | solution.py:17
  565.6 28.9 %collective-permute-start.3 = (bf16[384,2,128]{2,0,1:T(8,128)(2,1)}, bf16[384,2,128]{2,0,1:T(8,128)(2,1)}, u32[]{:S(2)}, u32[]{:S(2)}) collective-permute-start(bf16[384,2,128]{2,0,1:T(8,128)(2,1)} %copy.192), channel_id=1, source_target_pairs={{7,0},{0,1},{1,2},{2,3},{3,4},{4,5},{5,6},{6,7},{15,8},{8,9},{9,10... | collective-permute-start | bytes 589832 | tf_op jit(solution)/shard_map/while/body/eval_jaxpr/ppermute | solution.py:17
  604.0 28.8 %collective-permute-start.4 = (f32[384,2,128]{2,0,1:T(8,128)}, f32[384,2,128]{2,0,1:T(8,128)}, u32[]{:S(2)}, u32[]{:S(2)}) collective-permute-start(f32[384,2,128]{2,0,1:T(8,128)} %fusion.268), channel_id=1, source_target_pairs={{7,0},{0,1},{1,2},{2,3},{3,4},{4,5},{5,6},{6,7},{15,8},{8,9},{9,10... | collective-permute-start | bytes 1179656 | tf_op jit(solution)/shard_map/while/body/eval_jaxpr/ppermute | solution.py:17
  606.1 26.7 %collective-permute-start.5 = (f32[384,2,128]{2,0,1:T(8,128)}, f32[384,2,128]{2,0,1:T(8,128)}, u32[]{:S(2)}, u32[]{:S(2)}) collective-permute-start(f32[384,2,128]{2,0,1:T(8,128)} %fusion.269), channel_id=1, source_target_pairs={{7,0},{0,1},{1,2},{2,3},{3,4},{4,5},{5,6},{6,7},{15,8},{8,9},{9,10... | collective-permute-start | bytes 1179656 | tf_op jit(solution)/shard_map/while/body/eval_jaxpr/ppermute | solution.py:17
  606.1 24.6 %collective-permute-start.2 = (bf16[384,2,128]{2,0,1:T(8,128)(2,1)}, bf16[384,2,128]{2,0,1:T(8,128)(2,1)}, u32[]{:S(2)}, u32[]{:S(2)}) collective-permute-start(bf16[384,2,128]{2,0,1:T(8,128)(2,1)} %copy.191), channel_id=1, source_target_pairs={{7,0},{0,1},{1,2},{2,3},{3,4},{4,5},{5,6},{6,7},{15,8},{8,9},{9,10... | collective-permute-start | bytes 589832 | tf_op jit(solution)/shard_map/while/body/eval_jaxpr/ppermute | solution.py:17
  606.1 26.7 %collective-permute-start.3 = (bf16[384,2,128]{2,0,1:T(8,128)(2,1)}, bf16[384,2,128]{2,0,1:T(8,128)(2,1)}, u32[]{:S(2)}, u32[]{:S(2)}) collective-permute-start(bf16[384,2,128]{2,0,1:T(8,128)(2,1)} %copy.192), channel_id=1, source_target_pairs={{7,0},{0,1},{1,2},{2,3},{3,4},{4,5},{5,6},{6,7},{15,8},{8,9},{9,10... | collective-permute-start | bytes 589832 | tf_op jit(solution)/shard_map/while/body/eval_jaxpr/ppermute | solution.py:17
  642.3 27.9 %collective-permute-start.4 = (f32[384,2,128]{2,0,1:T(8,128)}, f32[384,2,128]{2,0,1:T(8,128)}, u32[]{:S(2)}, u32[]{:S(2)}) collective-permute-start(f32[384,2,128]{2,0,1:T(8,128)} %fusion.268), channel_id=1, source_target_pairs={{7,0},{0,1},{1,2},{2,3},{3,4},{4,5},{5,6},{6,7},{15,8},{8,9},{9,10... | collective-permute-start | bytes 1179656 | tf_op jit(solution)/shard_map/while/body/eval_jaxpr/ppermute | solution.py:17
  644.4 25.8 %collective-permute-start.5 = (f32[384,2,128]{2,0,1:T(8,128)}, f32[384,2,128]{2,0,1:T(8,128)}, u32[]{:S(2)}, u32[]{:S(2)}) collective-permute-start(f32[384,2,128]{2,0,1:T(8,128)} %fusion.269), channel_id=1, source_target_pairs={{7,0},{0,1},{1,2},{2,3},{3,4},{4,5},{5,6},{6,7},{15,8},{8,9},{9,10... | collective-permute-start | bytes 1179656 | tf_op jit(solution)/shard_map/while/body/eval_jaxpr/ppermute | solution.py:17
  644.4 25.8 %collective-permute-start.3 = (bf16[384,2,128]{2,0,1:T(8,128)(2,1)}, bf16[384,2,128]{2,0,1:T(8,128)(2,1)}, u32[]{:S(2)}, u32[]{:S(2)}) collective-permute-start(bf16[384,2,128]{2,0,1:T(8,128)(2,1)} %copy.192), channel_id=1, source_target_pairs={{7,0},{0,1},{1,2},{2,3},{3,4},{4,5},{5,6},{6,7},{15,8},{8,9},{9,10... | collective-permute-start | bytes 589832 | tf_op jit(solution)/shard_map/while/body/eval_jaxpr/ppermute | solution.py:17
  679.7 27.1 %collective-permute-start.4 = (f32[384,2,128]{2,0,1:T(8,128)}, f32[384,2,128]{2,0,1:T(8,128)}, u32[]{:S(2)}, u32[]{:S(2)}) collective-permute-start(f32[384,2,128]{2,0,1:T(8,128)} %fusion.268), channel_id=1, source_target_pairs={{7,0},{0,1},{1,2},{2,3},{3,4},{4,5},{5,6},{6,7},{15,8},{8,9},{9,10... | collective-permute-start | bytes 1179656 | tf_op jit(solution)/shard_map/while/body/eval_jaxpr/ppermute | solution.py:17
  681.8 25.0 %collective-permute-start.5 = (f32[384,2,128]{2,0,1:T(8,128)}, f32[384,2,128]{2,0,1:T(8,128)}, u32[]{:S(2)}, u32[]{:S(2)}) collective-permute-start(f32[384,2,128]{2,0,1:T(8,128)} %fusion.269), channel_id=1, source_target_pairs={{7,0},{0,1},{1,2},{2,3},{3,4},{4,5},{5,6},{6,7},{15,8},{8,9},{9,10... | collective-permute-start | bytes 1179656 | tf_op jit(solution)/shard_map/while/body/eval_jaxpr/ppermute | solution.py:17
  681.8 25.0 %collective-permute-start.3 = (bf16[384,2,128]{2,0,1:T(8,128)(2,1)}, bf16[384,2,128]{2,0,1:T(8,128)(2,1)}, u32[]{:S(2)}, u32[]{:S(2)}) collective-permute-start(bf16[384,2,128]{2,0,1:T(8,128)(2,1)} %copy.192), channel_id=1, source_target_pairs={{7,0},{0,1},{1,2},{2,3},{3,4},{4,5},{5,6},{6,7},{15,8},{8,9},{9,10... | collective-permute-start | bytes 589832 | tf_op jit(solution)/shard_map/while/body/eval_jaxpr/ppermute | solution.py:17
  716.2 26.2 %collective-permute-start.4 = (f32[384,2,128]{2,0,1:T(8,128)}, f32[384,2,128]{2,0,1:T(8,128)}, u32[]{:S(2)}, u32[]{:S(2)}) collective-permute-start(f32[384,2,128]{2,0,1:T(8,128)} %fusion.268), channel_id=1, source_target_pairs={{7,0},{0,1},{1,2},{2,3},{3,4},{4,5},{5,6},{6,7},{15,8},{8,9},{9,10... | collective-permute-start | bytes 1179656 | tf_op jit(solution)/shard_map/while/body/eval_jaxpr/ppermute | solution.py:17
  718.3 24.1 %collective-permute-start.5 = (f32[384,2,128]{2,0,1:T(8,128)}, f32[384,2,128]{2,0,1:T(8,128)}, u32[]{:S(2)}, u32[]{:S(2)}) collective-permute-start(f32[384,2,128]{2,0,1:T(8,128)} %fusion.269), channel_id=1, source_target_pairs={{7,0},{0,1},{1,2},{2,3},{3,4},{4,5},{5,6},{6,7},{15,8},{8,9},{9,10... | collective-permute-start | bytes 1179656 | tf_op jit(solution)/shard_map/while/body/eval_jaxpr/ppermute | solution.py:17
  718.3 24.1 %collective-permute-start.3 = (bf16[384,2,128]{2,0,1:T(8,128)(2,1)}, bf16[384,2,128]{2,0,1:T(8,128)(2,1)}, u32[]{:S(2)}, u32[]{:S(2)}) collective-permute-start(bf16[384,2,128]{2,0,1:T(8,128)(2,1)} %copy.192), channel_id=1, source_target_pairs={{7,0},{0,1},{1,2},{2,3},{3,4},{4,5},{5,6},{6,7},{15,8},{8,9},{9,10... | collective-permute-start | bytes 589832 | tf_op jit(solution)/shard_map/while/body/eval_jaxpr/ppermute | solution.py:17
  (87 other events, 3285.9 us)
Sparse Core Ops, SparseCore 0:
  210.1 120.7 reduce-scatter.6
  333.7 76.8 all-gather.2
  462.4 137.8 reduce-scatter.4
where the time goes:
time: 816 us; the launch traced here: 810 us
  blocking collectives  209 us (26%)
  waiting for transfers between devices  195 us (24%)
  other arithmetic  142 us (17%)
  matrix products  110 us (13%)
  local copies, waits for them, and re-layouts  96.7 us (12%)
  starting transfers between devices  40.9 us (5%)
  between operations  17 us (2%)
    ppermute x44, waiting for transfers between devices, from_behind(): return lax.ppermute(block, axis, route)  194 us
    unnamed x2, blocking collectives  132 us
    while x63, local copies, waits for them, and re-layouts  53.4 us
    concatenate x3, other arithmetic, per_device(): jnp.concatenate([first_half, second_half], axis=-1).astype(jnp.bfloat16)  49.8 us
    reduce_sum x1, other arithmetic, norm_backward(): centre = mixed - jnp.mean(mixed, axis=-1, keepdims=True)  43.8 us
    all_gather x1, blocking collectives, per_device(): lax.all_gather(kernel, 'dp', axis=0, tiled=True)  41.1 us
    psum x1, blocking collectives, per_device(): lax.psum((proj_part, kernel_part, gain_part), 'tm')  35.7 us
    reduce_sum x4, other arithmetic, tap_products(): jnp.sum(grad_f * padded[tap:tap + frame_rows].astype(jnp.float32), axis=0)  28 us
  transfers between devices with their start and end apart: 51, of which 27 were waited for; matrix products, arithmetic and copies ran while one was open for 30% of the time, Pallas kernels for 0%

commit v1 on v0

--- a/solution.py
+++ b/solution.py
@@ -102,7 +102,9 @@
     length = lengths[0]
     full_proj, full_kernel, full_gain = (
         lax.all_gather(projection, "dp", axis=0, tiled=True),
-        lax.all_gather(kernel, "dp", axis=0, tiled=True),
+        jnp.concatenate(
+            lax.all_to_all(jnp.stack([kernel] * lax.axis_size("dp")), "dp", 0, 0), axis=0
+        ),
         lax.all_gather(norm_gain, "dp", axis=0, tiled=True),
     )
     query_heads = queries[0].reshape(frame_rows, HEADS, HDIM)

time: 816 us -> 776 us (0.951)
  blocking collectives: 209 us -> 163 us
  starting transfers between devices: 40.9 us -> 53.8 us
    all_gather x1 -> x0, blocking collectives: 41.1 us -> none  [per_device(): lax.all_gather(kernel, 'dp', axis=0, tiled=True)]
    all_to_all x0 -> x1, starting transfers between devices: none -> 11.6 us  [per_device(): lax.all_to_all(jnp.stack([kernel] * lax.axis_size('dp')), 'dp', 0, 0)]
    ppermute x44, starting transfers between devices: 20.5 us -> 31 us  [from_behind(): return lax.ppermute(block, axis, route)]
    reduce_scatter x1, starting transfers between devices: 9.55 us -> 0.21 us  [per_device(): lax.psum_scatter(lax.dot_general(upstream_rows, attended_flat, (((0,), (0...]
    unnamed x127 -> x188, local copies, waits for them, and re-layouts: 24.8 us -> 26.5 us
  transfers between devices with their start and end apart: 51 -> 52, of which waited for: 27 -> 26; matrix products, arithmetic and copies ran while one was open for 30% -> 31% of each run, Pallas kernels for 0% -> 0%
where the time goes in v1:
time: 776 us; the launch traced here: 768 us
  waiting for transfers between devices  191 us (25%)
  blocking collectives  163 us (21%)
  other arithmetic  136 us (18%)
  matrix products  110 us (14%)
  local copies, waits for them, and re-layouts  97 us (12%)
  starting transfers between devices  53.8 us (7%)
  between operations  17.3 us (2%)
    ppermute x44, waiting for transfers between devices, from_behind(): return lax.ppermute(block, axis, route)  190 us
    unnamed x2, blocking collectives  128 us
    while x63, local copies, waits for them, and re-layouts  53.4 us
    concatenate x3, other arithmetic, per_device(): jnp.concatenate([first_half, second_half], axis=-1).astype(jnp.bfloat16)  45.9 us
    reduce_sum x1, other arithmetic, norm_backward(): centre = mixed - jnp.mean(mixed, axis=-1, keepdims=True)  41.9 us
    psum x1, blocking collectives, per_device(): lax.psum((proj_part, kernel_part, gain_part), 'tm')  35.6 us
    ppermute x44, starting transfers between devices, from_behind(): return lax.ppermute(block, axis, route)  31 us
    reduce_sum x4, other arithmetic, tap_products(): jnp.sum(grad_f * padded[tap:tap + frame_rows].astype(jnp.float32), axis=0)  27.9 us
  transfers between devices with their start and end apart: 52, of which 26 were waited for; matrix products, arithmetic and copies ran while one was open for 31% of the time, Pallas kernels for 0%

profile of v1, /device:TPU:4, one launch (start us, length us, event | category | flops | bytes accessed | tf_op | source)
XLA Modules:
  0.0 768.0 jit_solution(11246165425404114610)
XLA Ops:
  8.9 11.6 %all-to-all-start = ((bf16[32,2,992]{2,1,0:T(2,128)(2,1)}), bf16[32,2,992]{2,1,0:T(2,128)(2,1)}, u32[]{:S(2)}, u32[]{:S(2)}) async-start(bf16[32,2,992]{2,1,0:T(2,128)(2,1)} %reshape.197), calls=%async_computation.1 | async-start | bytes 262144 | tf_op jit(solution)/shard_map/all_to_all | solution.py:106
  32.0 64.3 %all-reduce = bf16[2048]{0:T(1024)(128)(2,1)S(1)} all-reduce(bf16[2048]{0:T(1024)(128)(2,1)S(1)} %dynamic-update-slice), channel_id=1, replica_groups=mesh['dp'=32,'tm'=8] {'dp'}, use_global_device_ids=true, to_apply=%add | all-reduce | flops 2048 | bytes 8192
  100.2 41.9 %fusion.190 = (f32[384]{0:T(512)S(1)}, f32[384,2048]{1,0:T(8,128)S(1)}) fusion(f32[2048]{0:T(1024)S(1)} %bitcast.232, bf16[15,2048]{1,0:T(8,128)(2,1)S(1)} %collective-permute-done.9, bf16[384,2048]{1,0:T(8,128)(2,1)} %copy-done.3, f32[2048]{0:T(1024)S(1)} %bitcast.234, f32[2048]{0:T(1024)S(1)} %bitcast.236, f32[2048]{0:T(1024)S(1)} %bitcast.238, ...), kind=kLoop, calls=%fused_computation.373 | loop fusion | flops 143916672 | bytes 5096960 | tf_op jit(solution)/shard_map/reduce_sum | solution.py:67
  146.1 12.3 %fusion.98 = (f32[2048]{0:T(1024)}, f32[2048]{0:T(1024)}, f32[2048]{0:T(1024)}, f32[2048]{0:T(1024)}, f32[2048]{0:T(1024)}, /*index=5*/f32[2048]{0:T(1024)}, f32...) fusion(bf16[15,2048]{1,0:T(8,128)(2,1)S(1)} %collective-permute-done.9, ...), kind=kLoop, calls=%fused_computation.234 | loop fusion | flops 49526784 | bytes 9586688 | tf_op jit(solution)/shard_map/reduce_sum | solution.py:59
  158.4 7.3 fusion.97
  165.7 4.7 fusion.82
  170.5 3.6 fusion.81
  174.1 3.5 stack.163
  191.9 95.2 %while.48 = (s32[]{:T(128)}, bf16[384,2,128]{2,0,1:T(8,128)(2,1)}, bf16[384,2,128]{2,0,1:T(8,128)(2,1)}, f32[2,384]{1,0:T(2,128)S(1)}, f32[2,384]{1,0:T(2,128)S(...) while((s32[]{:T(128)}, bf16[384,2,128]{2,0,1:T(8,128)(2,1)}, ...), condition=%wide.region_3.4_spmd.clone, body=%wide.region_0.3_spmd.clone.sunk | while | flops 530552064 | bytes 12043402 | solution.py:151
  201.8 3.2 fusion.255
  212.9 3.3 fusion.255
  225.5 3.3 fusion.255
  237.8 3.3 fusion.255
  243.5 4.2 collective-permute-done.1
  253.3 3.3 fusion.255
  258.6 3.4 collective-permute-done.1
  266.8 3.3 fusion.255
  280.2 3.3 fusion.255
  292.7 5.2 collective-permute-start.11
  301.1 63.2 %all-reduce.1 = f32[2048]{0:T(1024)} all-reduce(f32[2048]{0:T(1024)} %get-tuple-element.733), channel_id=4, replica_groups=mesh['dp'=32,'tm'=8] {'dp'}, use_global_device_ids=true, to_apply=%region_48.49.clone | all-reduce | flops 2048 | bytes 16384
  365.9 42.8 %fusion.104 = (bf16[1,384,2048]{2,1,0:T(8,128)(2,1)S(1)}, f32[384,2048]{1,0:T(8,128)S(1)}) fusion(bf16[384,4096]{1,0:T(8,128)(2,1)} %bitcast.215, f32[384]{0:T(512)S(1)} %copy-done.78, f32[2048]{0:T(1024)S(1)} %bitcast.233, bf16[384,2048]{1,0:T(8,128)(2,1)} %copy-done.5, bf16[15,2048]{1,0:T(8,128)(2,1)} %collective-permute-done.11, f32[2048]{0:T(1024)S(1)} %bitcast.235, ...), kind=kLoop, calls=%fused_computation.250 | loop fusion | flops 148635648 | bytes 8242688 | tf_op jit(solution)/shard_map/concatenate | solution.py:230
  418.2 3.2 convolution_bitcast_fusion.4
  424.1 276.9 %while.49 = (s32[]{:T(128)}, bf16[384,2,128]{2,0,1:T(8,128)(2,1)}, bf16[384,2,128]{2,0,1:T(8,128)(2,1)}, f32[384,2,128]{2,0,1:T(8,128)}, f32[384,2,128]{2,0,1:T(...) while((s32[]{:T(128)}, bf16[384,2,128]{2,0,1:T(8,128)(2,1)}, ...), condition=%wide.region_7.8_spmd.clone, body=%wide.region_6.7_spmd.clone.sunk | while | flops 380240640 | bytes 16915696 | solution.py:200
  443.8 17.0 %collective-permute-done.2 = bf16[384,2,128]{2,0,1:T(8,128)(2,1)} collective-permute-done((bf16[384,2,128]{2,0,1:T(8,128)(2,1)}, bf16[384,2,128]{2,0,1:T(8,128)(2,1)}, u32[]{:S(2)}, u32[]{:S(2)}) %collective-permute-start.2) | collective-permute-done | bytes 196640 | tf_op jit(solution)/shard_map/while/body/eval_jaxpr/ppermute | solution.py:17
  482.5 26.3 %collective-permute-done.2 = bf16[384,2,128]{2,0,1:T(8,128)(2,1)} collective-permute-done((bf16[384,2,128]{2,0,1:T(8,128)(2,1)}, bf16[384,2,128]{2,0,1:T(8,128)(2,1)}, u32[]{:S(2)}, u32[]{:S(2)}) %collective-permute-start.2) | collective-permute-done | bytes 196640 | tf_op jit(solution)/shard_map/while/body/eval_jaxpr/ppermute | solution.py:17
  508.8 3.5 collective-permute-done.3
  529.9 20.3 %collective-permute-done.2 = bf16[384,2,128]{2,0,1:T(8,128)(2,1)} collective-permute-done((bf16[384,2,128]{2,0,1:T(8,128)(2,1)}, bf16[384,2,128]{2,0,1:T(8,128)(2,1)}, u32[]{:S(2)}, u32[]{:S(2)}) %collective-permute-start.2) | collective-permute-done | bytes 196640 | tf_op jit(solution)/shard_map/while/body/eval_jaxpr/ppermute | solution.py:17
  569.4 19.7 %collective-permute-done.2 = bf16[384,2,128]{2,0,1:T(8,128)(2,1)} collective-permute-done((bf16[384,2,128]{2,0,1:T(8,128)(2,1)}, bf16[384,2,128]{2,0,1:T(8,128)(2,1)}, u32[]{:S(2)}, u32[]{:S(2)}) %collective-permute-start.2) | collective-permute-done | bytes 196640 | tf_op jit(solution)/shard_map/while/body/eval_jaxpr/ppermute | solution.py:17
  606.6 20.0 %collective-permute-done.2 = bf16[384,2,128]{2,0,1:T(8,128)(2,1)} collective-permute-done((bf16[384,2,128]{2,0,1:T(8,128)(2,1)}, bf16[384,2,128]{2,0,1:T(8,128)(2,1)}, u32[]{:S(2)}, u32[]{:S(2)}) %collective-permute-start.2) | collective-permute-done | bytes 196640 | tf_op jit(solution)/shard_map/while/body/eval_jaxpr/ppermute | solution.py:17
  642.9 20.2 %collective-permute-done.2 = bf16[384,2,128]{2,0,1:T(8,128)(2,1)} collective-permute-done((bf16[384,2,128]{2,0,1:T(8,128)(2,1)}, bf16[384,2,128]{2,0,1:T(8,128)(2,1)}, u32[]{:S(2)}, u32[]{:S(2)}) %collective-permute-start.2) | collective-permute-done | bytes 196640 | tf_op jit(solution)/shard_map/while/body/eval_jaxpr/ppermute | solution.py:17
  679.2 19.7 %collective-permute-done.2 = bf16[384,2,128]{2,0,1:T(8,128)(2,1)} collective-permute-done((bf16[384,2,128]{2,0,1:T(8,128)(2,1)}, bf16[384,2,128]{2,0,1:T(8,128)(2,1)}, u32[]{:S(2)}, u32[]{:S(2)}) %collective-permute-start.2) | collective-permute-done | bytes 196640 | tf_op jit(solution)/shard_map/while/body/eval_jaxpr/ppermute | solution.py:17
  724.9 35.6 %all-reduce.4 = (bf16[128,256]{0,1:T(8,128)(2,1)S(1)}, f32[64,31]{0,1:T(8,128)}, f32[64]{0:T(128)}) all-reduce(f32[128,256]{0,1:T(8,128)} %reduce-scatter.5.cloned.1.call-done, f32[64,31]{0,1:T(8,128)S(1)} %copy-done.71, f32[64]{0:T(128)} %dynamic-slice.2), channel_id=1, replica_groups=mesh['dp'=32,'tm'=8] {'tm'}, use_global_device_ids=true, to_apply=%region_9.10 | all-reduce | flops 34816 | bytes 212992 | tf_op jit(solution)/shard_map/psum | solution.py:247
  (462 shorter events, 273.1 us)
Async XLA Ops:
  8.9 87.4 %all-to-all-start = ((bf16[32,2,992]{2,1,0:T(2,128)(2,1)}), bf16[32,2,992]{2,1,0:T(2,128)(2,1)}, u32[]{:S(2)}, u32[]{:S(2)}) async-start(bf16[32,2,992]{2,1,0:T(2,128)(2,1)} %reshape.197), calls=%async_computation.1 | async-start | bytes 262144 | tf_op jit(solution)/shard_map/all_to_all | solution.py:106
  20.6 391.2 %reduce-scatter.7.cloned.1.call-start = ((), (), s32[]{:S(2)}) async-start(), calls=%async_computation.5 | async-start | bytes 1081344
  26.0 74.1 %collective-permute-start.8 = (bf16[15,2048]{1,0:T(8,128)(2,1)}, bf16[15,2048]{1,0:T(8,128)(2,1)S(1)}, u32[]{:S(2)}, u32[]{:S(2)}) collective-permute-start(bf16[15,2048]{1,0:T(8,128)(2,1)} %get-tuple-element.826), channel_id=1, source_target_pairs={{0,1},{1,2},{2,3},{3,4},{4,5},{5,6},{6,7},{8,9},{9,10},{10,11},{11... | collective-permute-start | bytes 184328 | tf_op jit(solution)/shard_map/ppermute | solution.py:28
  29.1 71.0 %collective-permute-start.9 = (bf16[15,2048]{1,0:T(8,128)(2,1)}, bf16[15,2048]{1,0:T(8,128)(2,1)S(1)}, u32[]{:S(2)}, u32[]{:S(2)}) collective-permute-start(bf16[15,2048]{1,0:T(8,128)(2,1)} %get-tuple-element.827), channel_id=1, source_target_pairs={{1,0},{2,1},{3,2},{4,3},{5,4},{6,5},{7,6},{9,8},{10,9},{11,10},{12... | collective-permute-start | bytes 184328 | tf_op jit(solution)/shard_map/ppermute | solution.py:30
  178.9 234.4 %all-gather.2.cloned.1.call-start = ((), (), s32[]{:S(2)}) async-start(), calls=%async_computation.3 | async-start | bytes 2162688 | tf_op jit(solution)/shard_map/all_gather | solution.py:104
  179.7 545.2 %reduce-scatter.5.cloned.1.call-start = ((), (), s32[]{:S(2)}) async-start(), calls=%async_computation.4 | async-start | bytes 4325376 | tf_op jit(solution)/shard_map/reduce_scatter | solution.py:232
  291.4 74.2 %collective-permute-start.10 = (bf16[15,2048]{1,0:T(8,128)(2,1)}, bf16[15,2048]{1,0:T(8,128)(2,1)}, u32[]{:S(2)}, u32[]{:S(2)}) collective-permute-start(bf16[15,2048]{1,0:T(8,128)(2,1)} %get-tuple-element.824), channel_id=1, source_target_pairs={{1,0},{2,1},{3,2},{4,3},{5,4},{6,5},{7,6},{9,8},{10,9},{11,10},{12... | collective-permute-start | bytes 184328 | tf_op jit(solution)/shard_map/ppermute | solution.py:30
  292.7 72.9 %collective-permute-start.11 = (bf16[15,2048]{1,0:T(8,128)(2,1)}, bf16[15,2048]{1,0:T(8,128)(2,1)}, u32[]{:S(2)}, u32[]{:S(2)}) collective-permute-start(bf16[15,2048]{1,0:T(8,128)(2,1)} %get-tuple-element.825), channel_id=1, source_target_pairs={{0,1},{1,2},{2,3},{3,4},{4,5},{5,6},{6,7},{8,9},{9,10},{10,11},{11... | collective-permute-start | bytes 184328 | tf_op jit(solution)/shard_map/ppermute | solution.py:28
  433.8 30.1 %collective-permute-start.4 = (f32[384,2,128]{2,0,1:T(8,128)}, f32[384,2,128]{2,0,1:T(8,128)}, u32[]{:S(2)}, u32[]{:S(2)}) collective-permute-start(f32[384,2,128]{2,0,1:T(8,128)} %fusion.268), channel_id=1, source_target_pairs={{7,0},{0,1},{1,2},{2,3},{3,4},{4,5},{5,6},{6,7},{15,8},{8,9},{9,10... | collective-permute-start | bytes 1179656 | tf_op jit(solution)/shard_map/while/body/eval_jaxpr/ppermute | solution.py:17
  437.5 26.3 %collective-permute-start.5 = (f32[384,2,128]{2,0,1:T(8,128)}, f32[384,2,128]{2,0,1:T(8,128)}, u32[]{:S(2)}, u32[]{:S(2)}) collective-permute-start(f32[384,2,128]{2,0,1:T(8,128)} %fusion.269), channel_id=1, source_target_pairs={{7,0},{0,1},{1,2},{2,3},{3,4},{4,5},{5,6},{6,7},{15,8},{8,9},{9,10... | collective-permute-start | bytes 1179656 | tf_op jit(solution)/shard_map/while/body/eval_jaxpr/ppermute | solution.py:17
  473.3 39.0 %collective-permute-start.4 = (f32[384,2,128]{2,0,1:T(8,128)}, f32[384,2,128]{2,0,1:T(8,128)}, u32[]{:S(2)}, u32[]{:S(2)}) collective-permute-start(f32[384,2,128]{2,0,1:T(8,128)} %fusion.268), channel_id=1, source_target_pairs={{7,0},{0,1},{1,2},{2,3},{3,4},{4,5},{5,6},{6,7},{15,8},{8,9},{9,10... | collective-permute-start | bytes 1179656 | tf_op jit(solution)/shard_map/while/body/eval_jaxpr/ppermute | solution.py:17
  475.4 36.9 %collective-permute-start.5 = (f32[384,2,128]{2,0,1:T(8,128)}, f32[384,2,128]{2,0,1:T(8,128)}, u32[]{:S(2)}, u32[]{:S(2)}) collective-permute-start(f32[384,2,128]{2,0,1:T(8,128)} %fusion.269), channel_id=1, source_target_pairs={{7,0},{0,1},{1,2},{2,3},{3,4},{4,5},{5,6},{6,7},{15,8},{8,9},{9,10... | collective-permute-start | bytes 1179656 | tf_op jit(solution)/shard_map/while/body/eval_jaxpr/ppermute | solution.py:17
  477.6 31.2 %collective-permute-start.2 = (bf16[384,2,128]{2,0,1:T(8,128)(2,1)}, bf16[384,2,128]{2,0,1:T(8,128)(2,1)}, u32[]{:S(2)}, u32[]{:S(2)}) collective-permute-start(bf16[384,2,128]{2,0,1:T(8,128)(2,1)} %copy.225), channel_id=1, source_target_pairs={{7,0},{0,1},{1,2},{2,3},{3,4},{4,5},{5,6},{6,7},{15,8},{8,9},{9,10... | collective-permute-start | bytes 589832 | tf_op jit(solution)/shard_map/while/body/eval_jaxpr/ppermute | solution.py:17
  479.0 33.3 %collective-permute-start.3 = (bf16[384,2,128]{2,0,1:T(8,128)(2,1)}, bf16[384,2,128]{2,0,1:T(8,128)(2,1)}, u32[]{:S(2)}, u32[]{:S(2)}) collective-permute-start(bf16[384,2,128]{2,0,1:T(8,128)(2,1)} %copy.226), channel_id=1, source_target_pairs={{7,0},{0,1},{1,2},{2,3},{3,4},{4,5},{5,6},{6,7},{15,8},{8,9},{9,10... | collective-permute-start | bytes 589832 | tf_op jit(solution)/shard_map/while/body/eval_jaxpr/ppermute | solution.py:17
  521.7 31.1 %collective-permute-start.4 = (f32[384,2,128]{2,0,1:T(8,128)}, f32[384,2,128]{2,0,1:T(8,128)}, u32[]{:S(2)}, u32[]{:S(2)}) collective-permute-start(f32[384,2,128]{2,0,1:T(8,128)} %fusion.268), channel_id=1, source_target_pairs={{7,0},{0,1},{1,2},{2,3},{3,4},{4,5},{5,6},{6,7},{15,8},{8,9},{9,10... | collective-permute-start | bytes 1179656 | tf_op jit(solution)/shard_map/while/body/eval_jaxpr/ppermute | solution.py:17
  523.9 29.0 %collective-permute-start.5 = (f32[384,2,128]{2,0,1:T(8,128)}, f32[384,2,128]{2,0,1:T(8,128)}, u32[]{:S(2)}, u32[]{:S(2)}) collective-permute-start(f32[384,2,128]{2,0,1:T(8,128)} %fusion.269), channel_id=1, source_target_pairs={{7,0},{0,1},{1,2},{2,3},{3,4},{4,5},{5,6},{6,7},{15,8},{8,9},{9,10... | collective-permute-start | bytes 1179656 | tf_op jit(solution)/shard_map/while/body/eval_jaxpr/ppermute | solution.py:17
  524.6 25.6 %collective-permute-start.2 = (bf16[384,2,128]{2,0,1:T(8,128)(2,1)}, bf16[384,2,128]{2,0,1:T(8,128)(2,1)}, u32[]{:S(2)}, u32[]{:S(2)}) collective-permute-start(bf16[384,2,128]{2,0,1:T(8,128)(2,1)} %copy.225), channel_id=1, source_target_pairs={{7,0},{0,1},{1,2},{2,3},{3,4},{4,5},{5,6},{6,7},{15,8},{8,9},{9,10... | collective-permute-start | bytes 589832 | tf_op jit(solution)/shard_map/while/body/eval_jaxpr/ppermute | solution.py:17
  525.5 27.4 %collective-permute-start.3 = (bf16[384,2,128]{2,0,1:T(8,128)(2,1)}, bf16[384,2,128]{2,0,1:T(8,128)(2,1)}, u32[]{:S(2)}, u32[]{:S(2)}) collective-permute-start(bf16[384,2,128]{2,0,1:T(8,128)(2,1)} %copy.226), channel_id=1, source_target_pairs={{7,0},{0,1},{1,2},{2,3},{3,4},{4,5},{5,6},{6,7},{15,8},{8,9},{9,10... | collective-permute-start | bytes 589832 | tf_op jit(solution)/shard_map/while/body/eval_jaxpr/ppermute | solution.py:17
  562.3 28.8 %collective-permute-start.4 = (f32[384,2,128]{2,0,1:T(8,128)}, f32[384,2,128]{2,0,1:T(8,128)}, u32[]{:S(2)}, u32[]{:S(2)}) collective-permute-start(f32[384,2,128]{2,0,1:T(8,128)} %fusion.268), channel_id=1, source_target_pairs={{7,0},{0,1},{1,2},{2,3},{3,4},{4,5},{5,6},{6,7},{15,8},{8,9},{9,10... | collective-permute-start | bytes 1179656 | tf_op jit(solution)/shard_map/while/body/eval_jaxpr/ppermute | solution.py:17
  564.5 26.7 %collective-permute-start.5 = (f32[384,2,128]{2,0,1:T(8,128)}, f32[384,2,128]{2,0,1:T(8,128)}, u32[]{:S(2)}, u32[]{:S(2)}) collective-permute-start(f32[384,2,128]{2,0,1:T(8,128)} %fusion.269), channel_id=1, source_target_pairs={{7,0},{0,1},{1,2},{2,3},{3,4},{4,5},{5,6},{6,7},{15,8},{8,9},{9,10... | collective-permute-start | bytes 1179656 | tf_op jit(solution)/shard_map/while/body/eval_jaxpr/ppermute | solution.py:17
  564.5 24.6 %collective-permute-start.2 = (bf16[384,2,128]{2,0,1:T(8,128)(2,1)}, bf16[384,2,128]{2,0,1:T(8,128)(2,1)}, u32[]{:S(2)}, u32[]{:S(2)}) collective-permute-start(bf16[384,2,128]{2,0,1:T(8,128)(2,1)} %copy.225), channel_id=1, source_target_pairs={{7,0},{0,1},{1,2},{2,3},{3,4},{4,5},{5,6},{6,7},{15,8},{8,9},{9,10... | collective-permute-start | bytes 589832 | tf_op jit(solution)/shard_map/while/body/eval_jaxpr/ppermute | solution.py:17
  564.5 26.7 %collective-permute-start.3 = (bf16[384,2,128]{2,0,1:T(8,128)(2,1)}, bf16[384,2,128]{2,0,1:T(8,128)(2,1)}, u32[]{:S(2)}, u32[]{:S(2)}) collective-permute-start(bf16[384,2,128]{2,0,1:T(8,128)(2,1)} %copy.226), channel_id=1, source_target_pairs={{7,0},{0,1},{1,2},{2,3},{3,4},{4,5},{5,6},{6,7},{15,8},{8,9},{9,10... | collective-permute-start | bytes 589832 | tf_op jit(solution)/shard_map/while/body/eval_jaxpr/ppermute | solution.py:17
  600.6 28.0 %collective-permute-start.4 = (f32[384,2,128]{2,0,1:T(8,128)}, f32[384,2,128]{2,0,1:T(8,128)}, u32[]{:S(2)}, u32[]{:S(2)}) collective-permute-start(f32[384,2,128]{2,0,1:T(8,128)} %fusion.268), channel_id=1, source_target_pairs={{7,0},{0,1},{1,2},{2,3},{3,4},{4,5},{5,6},{6,7},{15,8},{8,9},{9,10... | collective-permute-start | bytes 1179656 | tf_op jit(solution)/shard_map/while/body/eval_jaxpr/ppermute | solution.py:17
  602.8 25.9 %collective-permute-start.5 = (f32[384,2,128]{2,0,1:T(8,128)}, f32[384,2,128]{2,0,1:T(8,128)}, u32[]{:S(2)}, u32[]{:S(2)}) collective-permute-start(f32[384,2,128]{2,0,1:T(8,128)} %fusion.269), channel_id=1, source_target_pairs={{7,0},{0,1},{1,2},{2,3},{3,4},{4,5},{5,6},{6,7},{15,8},{8,9},{9,10... | collective-permute-start | bytes 1179656 | tf_op jit(solution)/shard_map/while/body/eval_jaxpr/ppermute | solution.py:17
  602.8 23.8 %collective-permute-start.2 = (bf16[384,2,128]{2,0,1:T(8,128)(2,1)}, bf16[384,2,128]{2,0,1:T(8,128)(2,1)}, u32[]{:S(2)}, u32[]{:S(2)}) collective-permute-start(bf16[384,2,128]{2,0,1:T(8,128)(2,1)} %copy.225), channel_id=1, source_target_pairs={{7,0},{0,1},{1,2},{2,3},{3,4},{4,5},{5,6},{6,7},{15,8},{8,9},{9,10... | collective-permute-start | bytes 589832 | tf_op jit(solution)/shard_map/while/body/eval_jaxpr/ppermute | solution.py:17
  602.8 25.9 %collective-permute-start.3 = (bf16[384,2,128]{2,0,1:T(8,128)(2,1)}, bf16[384,2,128]{2,0,1:T(8,128)(2,1)}, u32[]{:S(2)}, u32[]{:S(2)}) collective-permute-start(bf16[384,2,128]{2,0,1:T(8,128)(2,1)} %copy.226), channel_id=1, source_target_pairs={{7,0},{0,1},{1,2},{2,3},{3,4},{4,5},{5,6},{6,7},{15,8},{8,9},{9,10... | collective-permute-start | bytes 589832 | tf_op jit(solution)/shard_map/while/body/eval_jaxpr/ppermute | solution.py:17
  638.1 27.1 %collective-permute-start.4 = (f32[384,2,128]{2,0,1:T(8,128)}, f32[384,2,128]{2,0,1:T(8,128)}, u32[]{:S(2)}, u32[]{:S(2)}) collective-permute-start(f32[384,2,128]{2,0,1:T(8,128)} %fusion.268), channel_id=1, source_target_pairs={{7,0},{0,1},{1,2},{2,3},{3,4},{4,5},{5,6},{6,7},{15,8},{8,9},{9,10... | collective-permute-start | bytes 1179656 | tf_op jit(solution)/shard_map/while/body/eval_jaxpr/ppermute | solution.py:17
  640.2 25.0 %collective-permute-start.5 = (f32[384,2,128]{2,0,1:T(8,128)}, f32[384,2,128]{2,0,1:T(8,128)}, u32[]{:S(2)}, u32[]{:S(2)}) collective-permute-start(f32[384,2,128]{2,0,1:T(8,128)} %fusion.269), channel_id=1, source_target_pairs={{7,0},{0,1},{1,2},{2,3},{3,4},{4,5},{5,6},{6,7},{15,8},{8,9},{9,10... | collective-permute-start | bytes 1179656 | tf_op jit(solution)/shard_map/while/body/eval_jaxpr/ppermute | solution.py:17
  640.2 25.0 %collective-permute-start.3 = (bf16[384,2,128]{2,0,1:T(8,128)(2,1)}, bf16[384,2,128]{2,0,1:T(8,128)(2,1)}, u32[]{:S(2)}, u32[]{:S(2)}) collective-permute-start(bf16[384,2,128]{2,0,1:T(8,128)(2,1)} %copy.226), channel_id=1, source_target_pairs={{7,0},{0,1},{1,2},{2,3},{3,4},{4,5},{5,6},{6,7},{15,8},{8,9},{9,10... | collective-permute-start | bytes 589832 | tf_op jit(solution)/shard_map/while/body/eval_jaxpr/ppermute | solution.py:17
  674.7 26.3 %collective-permute-start.4 = (f32[384,2,128]{2,0,1:T(8,128)}, f32[384,2,128]{2,0,1:T(8,128)}, u32[]{:S(2)}, u32[]{:S(2)}) collective-permute-start(f32[384,2,128]{2,0,1:T(8,128)} %fusion.268), channel_id=1, source_target_pairs={{7,0},{0,1},{1,2},{2,3},{3,4},{4,5},{5,6},{6,7},{15,8},{8,9},{9,10... | collective-permute-start | bytes 1179656 | tf_op jit(solution)/shard_map/while/body/eval_jaxpr/ppermute | solution.py:17
  676.8 24.2 %collective-permute-start.5 = (f32[384,2,128]{2,0,1:T(8,128)}, f32[384,2,128]{2,0,1:T(8,128)}, u32[]{:S(2)}, u32[]{:S(2)}) collective-permute-start(f32[384,2,128]{2,0,1:T(8,128)} %fusion.269), channel_id=1, source_target_pairs={{7,0},{0,1},{1,2},{2,3},{3,4},{4,5},{5,6},{6,7},{15,8},{8,9},{9,10... | collective-permute-start | bytes 1179656 | tf_op jit(solution)/shard_map/while/body/eval_jaxpr/ppermute | solution.py:17
  676.8 24.1 %collective-permute-start.3 = (bf16[384,2,128]{2,0,1:T(8,128)(2,1)}, bf16[384,2,128]{2,0,1:T(8,128)(2,1)}, u32[]{:S(2)}, u32[]{:S(2)}) collective-permute-start(bf16[384,2,128]{2,0,1:T(8,128)(2,1)} %copy.226), channel_id=1, source_target_pairs={{7,0},{0,1},{1,2},{2,3},{3,4},{4,5},{5,6},{6,7},{15,8},{8,9},{9,10... | collective-permute-start | bytes 589832 | tf_op jit(solution)/shard_map/while/body/eval_jaxpr/ppermute | solution.py:17
  (117 other events, 4341.1 us)
Sparse Core Ops, SparseCore 0:
  179.0 121.1 reduce-scatter.6
  303.0 76.6 all-gather.1
  421.6 137.0 reduce-scatter.4
